TPU v7x, 32 devices: a whole 2x2x4 slice. The times are simulated.
32 devices in a mesh: vox: 16 (over z, y, core), star: 2 (over x).
Axes of the slice: x: 2, y: 2, z: 4, core: 2. Of those that a mesh axis runs over, the one named last changes fastest.
Arguments:
- mean_field: float32 [32, 128, 128], P('vox', 'star'), may hold values from -3 to 3
- deviations: float32 [4, 32, 128, 128], P(None, 'vox', 'star'), may hold values from -4 to 4
- stencil: float32 [3, 3], replicated, may hold values from -2 to 2
- vertical_mix: float32 [128, 128], replicated, may hold values from -0.5 to 0.5
- log_mean: float32 [128], replicated, may hold values from -1.6 to -0.4
- responses: bfloat16 [3072, 128, 128], P(('vox', 'star')), may hold values from 0 to 0.015625
- pair_line: int32 [3072], P(('vox', 'star')), may hold values from 0 to 127
- pair_owner: int32 [3072, 1], P(('vox', 'star')), may hold values from 0 to 15; in each aligned block of 96 rows (0 to 95, 96 to 191, ...) at most 12 rows name the same one
- pair_star: int32 [3072], P(('vox', 'star')), may hold values from 0 to 7
- observed: float32 [256, 128], P(('vox', 'star')), may hold values from 0 to 15
- inv_var: float32 [256, 128], P(('vox', 'star')), may hold values from 0.05 to 0.5
Outputs:
- gradient: float32 [32, 128, 128], P('vox', 'star')
- residual_mean: float32 [256, 128], P(('vox', 'star'))
Inputs may be any that keep to these rules, and one draw needn't show every extreme that they name: `pair_owner`: among the 96 pairs of one device at most 12 name one owner, a bound that some block reaches.
All inputs are finite; a program needn't handle non-finite values.
Results may differ from a plain program's by a relative error of at most 0.0015.
Values may be sent and summed in bfloat16 or wider, within the bound.
No kernel may reach another device: no remote copies, remote signals or barrier semaphores. Data moves between devices by JAX's collectives and lax.ppermute only.
A program may use at most 64 MiB of HBM per device.

v0:
```python
import jax
import jax.numpy as jnp
from jax import lax
from jax.sharding import PartitionSpec as P

HIGH = lax.Precision.HIGHEST


def with_halo(cells, sides, width):
    for axis, dim in sides:
        count = lax.axis_size(axis)
        ends = count - 1
        head = lax.slice_in_dim(cells, 0, width, axis=dim)
        tail = lax.slice_in_dim(cells, cells.shape[dim] - width, cells.shape[dim], axis=dim)
        cells = jnp.concatenate(
            [
                lax.ppermute(tail, axis, [(i, (i + 1) % count) for i in range(ends)]),
                cells,
                lax.ppermute(head, axis, [((i + 1) % count, i) for i in range(ends)]),
            ],
            axis=dim,
        )
    return cells


def per_device(
    mean_field,
    deviations,
    stencil,
    vertical_mix,
    log_mean,
    responses,
    pair_line,
    pair_owner,
    pair_star,
    observed,
    inv_var,
):
    samples = deviations.shape[0]
    width_x = deviations.shape[1]
    width_y = deviations.shape[2]
    length = deviations.shape[3]
    pair_count = responses.shape[0]
    block_count = observed.shape[0]
    group_size = lax.axis_size("vox")
    latent = mean_field[None] + deviations
    padded = with_halo(latent, (("vox", 1), ("star", 2)), 1)
    smoothed = jnp.zeros(latent.shape, jnp.float32)
    for offset_x in range(3):
        for offset_y in range(3):
            smoothed = (
                smoothed
                + stencil[offset_x, offset_y]
                * padded[:, offset_x : offset_x + width_x, offset_y : offset_y + width_y, :]
            )
    log_density = jnp.einsum("sxyw,zw->sxyz", smoothed, vertical_mix, precision=HIGH) + log_mean
    density = jnp.exp(log_density)
    density_b = density.astype(jnp.bfloat16).reshape(samples, width_x * width_y, length)
    picked = jnp.take(density_b, pair_line, axis=1)
    contribution = jnp.einsum("pij,spj->psi", responses, picked, preferred_element_type=jnp.float32)
    star_count = observed.shape[0]
    group_blocks = group_size * star_count
    target = pair_owner[:, 0] * star_count + pair_star
    target_onehot = (target[:, None] == jnp.arange(group_blocks, dtype=jnp.int32)[None, :]).astype(
        jnp.float32
    )
    partial = jnp.einsum("pb,psi->bsi", target_onehot, contribution, precision=HIGH)
    extinction = lax.psum(partial, "vox")
    table = lax.all_gather(jnp.stack([observed, inv_var]), "vox", axis=1, tiled=True)
    misfit = table[1][:, None, :] * (extinction - table[0][:, None, :])
    misfit_b = misfit.astype(jnp.bfloat16)
    own = lax.dynamic_slice_in_dim(misfit, lax.axis_index("vox") * star_count, star_count, axis=0)
    residual_mean = jnp.mean(own, axis=1)
    pair_misfit = jnp.take(misfit_b, target, axis=0)
    pair_adjoint = jnp.einsum(
        "pij,psi->psj", responses, pair_misfit, preferred_element_type=jnp.float32
    )
    line_onehot = (
        pair_line[:, None] == jnp.arange(width_x * width_y, dtype=jnp.int32)[None, :]
    ).astype(jnp.float32)
    adjoint = jnp.einsum("pb,psj->sbj", line_onehot, pair_adjoint, precision=HIGH).reshape(
        samples, width_x, width_y, length
    )
    grad_log = density * adjoint
    grad_smooth = jnp.einsum("sxyz,zw->sxyw", grad_log, vertical_mix, precision=HIGH)
    padded_grad = with_halo(grad_smooth, (("vox", 1), ("star", 2)), 1)
    grad_latent = jnp.zeros(latent.shape, jnp.float32)
    for offset_x in range(3):
        for offset_y in range(3):
            grad_latent = (
                grad_latent
                + stencil[offset_x, offset_y]
                * padded_grad[
                    :,
                    2 - offset_x : 2 - offset_x + width_x,
                    2 - offset_y : 2 - offset_y + width_y,
                    :,
                ]
            )
    gradient = jnp.mean(grad_latent + latent, axis=0)
    return (gradient, residual_mean)


def solution(mesh):
    placed = (
        P("vox", "star", None),
        P(None, "vox", "star", None),
        P(),
        P(),
        P(),
        P(("vox", "star"), None, None),
        P(("vox", "star")),
        P(("vox", "star"), None),
        P(("vox", "star")),
        P(("vox", "star"), None),
        P(("vox", "star"), None),
    )
    return jax.shard_map(
        per_device,
        mesh=mesh,
        in_specs=placed,
        out_specs=(P("vox", "star", None), P(("vox", "star"), None)),
        check_vma=False,
    )
```

profile of v0, /device:TPU:7, one launch (start us, length us, event | category | flops | bytes accessed | tf_op | source)
XLA Modules:
  0.0 185.1 jit_solution(6022717707829478496)
XLA Ops:
  7.2 1.1 broadcast_add_fusion
  8.4 3.7 %collective-permute-start = (f32[4,1,64,128]{3,2,1,0:T(8,128)S(1)}, f32[4,1,64,128]{3,2,1,0:T(8,128)S(1)}, u32[]{:S(2)}, u32[]{:S(2)}) collective-permute-start(f32[4,1,64,128]{3,2,1,0:T(8,128)S(1)} %get-tuple-element.16), channel_id=1, source_target_pairs={{0,2},{2,4},{4,6},{6,8},{8,10},{10,12},{12,14},{14,16},{16,18},{18... | collective-permute-start | bytes 393224 | tf_op jit(solution)/shard_map/ppermute | solution.py:17
  12.1 1.9 %collective-permute-start.1 = (f32[4,1,64,128]{3,2,1,0:T(8,128)S(1)}, f32[4,1,64,128]{3,2,1,0:T(8,128)S(1)}, u32[]{:S(2)}, u32[]{:S(2)}) collective-permute-start(f32[4,1,64,128]{3,2,1,0:T(8,128)S(1)} %get-tuple-element.17), channel_id=1, source_target_pairs={{2,0},{4,2},{6,4},{8,6},{10,8},{12,10},{14,12},{16,14},{18,16},{20... | collective-permute-start | bytes 393224 | tf_op jit(solution)/shard_map/ppermute | solution.py:19
  14.0 0.7 compare_select_fusion
  14.7 0.7 pad_maximum_fusion.12
  15.4 19.6 %all_gather.3 = f32[2,128,128]{2,1,0:T(8,128)S(1)} all-gather(f32[2,8,128]{2,1,0:T(8,128)S(1)} %pad_maximum_fusion.12), channel_id=1, replica_groups=mesh['vox'=16,'star'=2] {'vox'}, dimensions={1}, use_global_device_ids=true | all-gather | bytes 139264 | tf_op jit(solution)/shard_map/all_gather | solution.py:69
  35.0 0.7 compare_and_fusion.1
  35.7 0.7 compare_and_fusion
  36.4 1.7 fusion.71
  38.1 1.3 collective-permute-start.2
  39.4 4.0 %collective-permute-start.3 = (f32[4,4,1,128]{3,2,1,0:T(1,128)S(1)}, f32[4,4,1,128]{3,2,1,0:T(1,128)S(1)}, u32[]{:S(2)}, u32[]{:S(2)}) collective-permute-start(f32[4,4,1,128]{3,2,1,0:T(1,128)S(1)} %get-tuple-element.13), channel_id=1, source_target_pairs={{1,0},{3,2},{5,4},{7,6},{9,8},{11,10},{13,12},{15,14},{17,16},{19,... | collective-permute-start | bytes 24584 | tf_op jit(solution)/shard_map/ppermute | solution.py:19
  43.4 0.8 collective-permute-done.3
  44.3 6.8 %fusion.72 = (bf16[4,2,64,128]{3,2,1,0:T(8,128)(2,1)S(1)}, f32[4,2,64,128]{3,2,1,0:T(8,128)}) fusion(f32[128]{0:T(128)S(1)} %copy-done.5, f32[128,128]{1,0:T(8,128)S(1)} %copy-done.2, f32[4,4,65,128]{3,2,1,0:T(8,128)S(1)} %get-tuple-element.11, f32[4,1,64,128]{3,2,1,0:T(8,128)S(1)} %collective-permute-done.1, f32[4,2,64,128]{3,2,1,0:T(8,128)S(1)} %broadcast_add_fusion, ...), kind=kOutput, calls=%fused_computation.109 | convolution fusion | flops 102039552 | bytes 2556452 | tf_op jit(solution)/shard_map/sxyw,zw->sxyz/dot_general | solution.py:56
  51.2 0.7 gather_fusion
  51.9 1.8 fusion.48
  53.7 1.1 fusion.37
  54.8 89.7 %all-reduce.2.cloned.1.call-done = f32[128,4,128]{2,0,1:T(8,128)} async-done(((f32[128,4,128]{2,0,1:T(8,128)}), f32[128,4,128]{2,0,1:T(8,128)}) %all-reduce.2.cloned.1.call-update) | async-done | bytes 262160 | tf_op jit(solution)/shard_map/psum | solution.py:68
  144.5 1.7 fusion.68
  146.3 0.7 gather_fusion.1
  147.0 1.0 fusion.51
  148.8 0.7 fusion.69
  149.6 5.3 %collective-permute-start.4 = (f32[4,1,64,128]{3,2,1,0:T(8,128)}, f32[4,1,64,128]{3,2,1,0:T(8,128)S(1)}, u32[]{:S(2)}, u32[]{:S(2)}) collective-permute-start(f32[4,1,64,128]{3,2,1,0:T(8,128)} %get-tuple-element.14), channel_id=1, source_target_pairs={{0,2},{2,4},{4,6},{6,8},{8,10},{10,12},{12,14},{14,16},{16,18},{18... | collective-permute-start | bytes 393224 | tf_op jit(solution)/shard_map/ppermute | solution.py:17
  154.8 1.9 %collective-permute-start.5 = (f32[4,1,64,128]{3,2,1,0:T(8,128)}, f32[4,1,64,128]{3,2,1,0:T(8,128)}, u32[]{:S(2)}, u32[]{:S(2)}) collective-permute-start(f32[4,1,64,128]{3,2,1,0:T(8,128)} %get-tuple-element.15), channel_id=1, source_target_pairs={{2,0},{4,2},{6,4},{8,6},{10,8},{12,10},{14,12},{16,14},{18,16},{20... | collective-permute-start | bytes 393224 | tf_op jit(solution)/shard_map/ppermute | solution.py:19
  156.8 0.7 dynamic-slice_reduce_fusion
  157.5 4.8 %collective-permute-done.5 = f32[4,1,64,128]{3,2,1,0:T(8,128)} collective-permute-done((f32[4,1,64,128]{3,2,1,0:T(8,128)}, f32[4,1,64,128]{3,2,1,0:T(8,128)}, u32[]{:S(2)}, u32[]{:S(2)}) %collective-permute-start.5) | collective-permute-done | bytes 131104 | tf_op jit(solution)/shard_map/ppermute | solution.py:19
  162.3 0.7 pad_maximum_fusion.8
  163.1 2.2 %collective-permute-start.6 = (f32[4,4,1,128]{3,2,1,0:T(1,128)S(1)}, f32[4,4,1,128]{3,2,1,0:T(1,128)S(1)}, u32[]{:S(2)}, u32[]{:S(2)}) collective-permute-start(f32[4,4,1,128]{3,2,1,0:T(1,128)S(1)} %get-tuple-element.8), channel_id=1, source_target_pairs={{1,0},{3,2},{5,4},{7,6},{9,8},{11,10},{13,12},{15,14},{17,16},{19,... | collective-permute-start | bytes 24584 | tf_op jit(solution)/shard_map/ppermute | solution.py:19
  165.3 1.3 collective-permute-start.7
  167.2 2.5 %collective-permute-done.7 = f32[4,4,1,128]{3,2,1,0:T(1,128)S(1)} collective-permute-done((f32[4,4,1,128]{3,2,1,0:T(1,128)S(1)}, f32[4,4,1,128]{3,2,1,0:T(1,128)S(1)}, u32[]{:S(2)}, u32[]{:S(2)}) %collective-permute-start.7) | collective-permute-done | bytes 8224 | tf_op jit(solution)/shard_map/ppermute | solution.py:17
  169.7 1.1 pad_maximum_fusion.1
  170.7 6.9 %fusion.3 = f32[2,64,128]{2,1,0:T(8,128)S(1)} fusion(f32[4,4,65,128]{3,2,1,0:T(8,128)S(1)} %get-tuple-element.7, f32[4,2,64,128]{3,2,1,0:T(8,128)S(1)} %fusion.32, f32[4,1,64,128]{3,2,1,0:T(8,128)S(1)} %collective-permute-done.4, f32[4,4,65,128]{3,2,1,0:T(8,128)S(1)} %get-tuple-element.6, f32[4,1,64,128]{3,2,1,0:T(8,128)} %collective-permute-done.5, ...), kind=kLoop, calls=%fused_computation.11 | loop fusion | flops 1425408 | bytes 2490404 | tf_op jit(solution)/shard_map/reduce_sum | solution.py:100
  177.6 0.6 broadcast_multiply_fusion
  (31 shorter events, 1.8 us)
Async XLA Ops:
  7.2 44.8 %copy-start = (bf16[96,128,128]{2,1,0:T(8,128)(2,1)S(1)}, bf16[96,128,128]{2,1,0:T(8,128)(2,1)}, u32[]{:S(2)}) copy-start(bf16[96,128,128]{2,1,0:T(8,128)(2,1)} %param.16) | copy-start | bytes 9437188
  7.2 37.1 %copy-start.2 = (f32[128,128]{1,0:T(8,128)S(1)}, f32[128,128]{1,0:T(8,128)}, u32[]{:S(2)}) copy-start(f32[128,128]{1,0:T(8,128)} %param.14) | copy-start | bytes 196612
  7.2 37.1 %copy-start.5 = (f32[128]{0:T(128)S(1)}, f32[128]{0:T(128)}, u32[]{:S(2)}) copy-start(f32[128]{0:T(128)} %param.15) | copy-start | bytes 1540
  7.2 137.3 %all-reduce.2.cloned.1.call-start = ((), (), s32[]{:S(2)}) async-start(), calls=%async_computation | async-start | bytes 524288 | tf_op jit(solution)/shard_map/psum | solution.py:68
  8.4 29.7 %collective-permute-start = (f32[4,1,64,128]{3,2,1,0:T(8,128)S(1)}, f32[4,1,64,128]{3,2,1,0:T(8,128)S(1)}, u32[]{:S(2)}, u32[]{:S(2)}) collective-permute-start(f32[4,1,64,128]{3,2,1,0:T(8,128)S(1)} %get-tuple-element.16), channel_id=1, source_target_pairs={{0,2},{2,4},{4,6},{6,8},{8,10},{10,12},{12,14},{14,16},{16,18},{18... | collective-permute-start | bytes 393224 | tf_op jit(solution)/shard_map/ppermute | solution.py:17
  12.1 26.0 %collective-permute-start.1 = (f32[4,1,64,128]{3,2,1,0:T(8,128)S(1)}, f32[4,1,64,128]{3,2,1,0:T(8,128)S(1)}, u32[]{:S(2)}, u32[]{:S(2)}) collective-permute-start(f32[4,1,64,128]{3,2,1,0:T(8,128)S(1)} %get-tuple-element.17), channel_id=1, source_target_pairs={{2,0},{4,2},{6,4},{8,6},{10,8},{12,10},{14,12},{16,14},{18,16},{20... | collective-permute-start | bytes 393224 | tf_op jit(solution)/shard_map/ppermute | solution.py:19
  38.1 5.3 %collective-permute-start.2 = (f32[4,4,1,128]{3,2,1,0:T(1,128)S(1)}, f32[4,4,1,128]{3,2,1,0:T(1,128)S(1)}, u32[]{:S(2)}, u32[]{:S(2)}) collective-permute-start(f32[4,4,1,128]{3,2,1,0:T(1,128)S(1)} %get-tuple-element.12), channel_id=1, source_target_pairs={{0,1},{2,3},{4,5},{6,7},{8,9},{10,11},{12,13},{14,15},{16,17},{18,... | collective-permute-start | bytes 24584 | tf_op jit(solution)/shard_map/ppermute | solution.py:17
  39.4 4.8 %collective-permute-start.3 = (f32[4,4,1,128]{3,2,1,0:T(1,128)S(1)}, f32[4,4,1,128]{3,2,1,0:T(1,128)S(1)}, u32[]{:S(2)}, u32[]{:S(2)}) collective-permute-start(f32[4,4,1,128]{3,2,1,0:T(1,128)S(1)} %get-tuple-element.13), channel_id=1, source_target_pairs={{1,0},{3,2},{5,4},{7,6},{9,8},{11,10},{13,12},{15,14},{17,16},{19,... | collective-permute-start | bytes 24584 | tf_op jit(solution)/shard_map/ppermute | solution.py:19
  53.7 94.3 %copy-start.4 = (s32[96]{0:T(128)S(1)}, s32[96]{0:T(128)}, u32[]{:S(2)}) copy-start(s32[96]{0:T(128)} %param.17) | copy-start | bytes 1156
  53.7 94.7 %copy-start.3 = (f32[128,128]{1,0:T(8,128)S(1)}, f32[128,128]{1,0:T(8,128)}, u32[]{:S(2)}) copy-start(f32[128,128]{1,0:T(8,128)} %param.14) | copy-start | bytes 196612
  147.0 1.4 copy-start.1
  149.6 7.9 %collective-permute-start.4 = (f32[4,1,64,128]{3,2,1,0:T(8,128)}, f32[4,1,64,128]{3,2,1,0:T(8,128)S(1)}, u32[]{:S(2)}, u32[]{:S(2)}) collective-permute-start(f32[4,1,64,128]{3,2,1,0:T(8,128)} %get-tuple-element.14), channel_id=1, source_target_pairs={{0,2},{2,4},{4,6},{6,8},{8,10},{10,12},{12,14},{14,16},{16,18},{18... | collective-permute-start | bytes 393224 | tf_op jit(solution)/shard_map/ppermute | solution.py:17
  154.8 7.5 %collective-permute-start.5 = (f32[4,1,64,128]{3,2,1,0:T(8,128)}, f32[4,1,64,128]{3,2,1,0:T(8,128)}, u32[]{:S(2)}, u32[]{:S(2)}) collective-permute-start(f32[4,1,64,128]{3,2,1,0:T(8,128)} %get-tuple-element.15), channel_id=1, source_target_pairs={{2,0},{4,2},{6,4},{8,6},{10,8},{12,10},{14,12},{16,14},{18,16},{20... | collective-permute-start | bytes 393224 | tf_op jit(solution)/shard_map/ppermute | solution.py:19
  163.1 4.1 %collective-permute-start.6 = (f32[4,4,1,128]{3,2,1,0:T(1,128)S(1)}, f32[4,4,1,128]{3,2,1,0:T(1,128)S(1)}, u32[]{:S(2)}, u32[]{:S(2)}) collective-permute-start(f32[4,4,1,128]{3,2,1,0:T(1,128)S(1)} %get-tuple-element.8), channel_id=1, source_target_pairs={{1,0},{3,2},{5,4},{7,6},{9,8},{11,10},{13,12},{15,14},{17,16},{19,... | collective-permute-start | bytes 24584 | tf_op jit(solution)/shard_map/ppermute | solution.py:19
  165.3 4.4 %collective-permute-start.7 = (f32[4,4,1,128]{3,2,1,0:T(1,128)S(1)}, f32[4,4,1,128]{3,2,1,0:T(1,128)S(1)}, u32[]{:S(2)}, u32[]{:S(2)}) collective-permute-start(f32[4,4,1,128]{3,2,1,0:T(1,128)S(1)} %get-tuple-element.9), channel_id=1, source_target_pairs={{0,1},{2,3},{4,5},{6,7},{8,9},{10,11},{12,13},{14,15},{16,17},{18,... | collective-permute-start | bytes 24584 | tf_op jit(solution)/shard_map/ppermute | solution.py:17
Sparse Core Ops, SparseCore 0:
  54.9 89.5 all-reduce.1
where the time goes:
time: 186 us; the launch traced here: 185 us
  waiting for transfers between devices  97.8 us (53%)
  starting transfers between devices  21.6 us (12%)
  blocking collectives  19.6 us (11%)
  other arithmetic  16.3 us (9%)
  between operations  14.3 us (8%)
  matrix products  11.4 us (6%)
  local copies, waits for them, and re-layouts  4.09 us (2%)
    psum x1, waiting for transfers between devices, per_device(): extinction = lax.psum(partial, 'vox')  89.7 us
    all_gather x1, blocking collectives, per_device(): lax.all_gather(jnp.stack([observed, inv_var]), 'vox', axis=1, tiled=True)  19.6 us
    ppermute x4, starting transfers between devices, with_halo(): lax.ppermute(tail, axis, [(i, (i + 1) % count) for i in range(ends)])  11.6 us
    ppermute x4, starting transfers between devices, with_halo(): lax.ppermute(head, axis, [((i + 1) % count, i) for i in range(ends)])  10 us
    reduce_sum x1, other arithmetic, per_device(): gradient = jnp.mean(grad_latent + latent, axis=0)  6.87 us
    dot_general x1, matrix products, per_device(): jnp.einsum('sxyw,zw->sxyz', smoothed, vertical_mix, precision=HIGH)  6.84 us
    ppermute x4, waiting for transfers between devices, with_halo(): lax.ppermute(head, axis, [((i + 1) % count, i) for i in range(ends)])  5.59 us
  transfers between devices with their start and end apart: 9, of which 4 were waited for; matrix products, arithmetic and copies ran while one was open for 3% of the time, Pallas kernels for 0%

commit v1 on v0

--- a/solution.py
+++ b/solution.py
@@ -66,7 +66,17 @@
     )
     partial = jnp.einsum("pb,psi->bsi", target_onehot, contribution, precision=HIGH)
     extinction = lax.psum(partial, "vox")
-    table = lax.all_gather(jnp.stack([observed, inv_var]), "vox", axis=1, tiled=True)
+    shard = jnp.stack([observed, inv_var])
+    ways = lax.axis_size("vox")
+    up = [(d, (d + 1) % ways) for d in range(ways)]
+    down = [(d, (d - 1) % ways) for d in range(ways)]
+    earlier, later = ([shard], [shard])
+    for _ in range(ways // 2):
+        earlier.append(lax.ppermute(earlier[-1], "vox", up))
+    for _ in range((ways - 1) // 2):
+        later.append(lax.ppermute(later[-1], "vox", down))
+    line = jnp.concatenate([*earlier[::-1], *later[1:]], axis=1)
+    table = jnp.roll(line, (lax.axis_index("vox") - ways // 2) * shard.shape[1], axis=1)
     misfit = table[1][:, None, :] * (extinction - table[0][:, None, :])
     misfit_b = misfit.astype(jnp.bfloat16)
     own = lax.dynamic_slice_in_dim(misfit, lax.axis_index("vox") * star_count, star_count, axis=0)

time: 186 us -> 224 us (1.20)
  the two profiles are of different devices: /device:TPU:7 before, /device:TPU:10 now
where the time goes in v1:
time: 224 us; the launch traced here: 222 us
  waiting for transfers between devices  110 us (49%)
  starting transfers between devices  39.3 us (18%)
  local copies, waits for them, and re-layouts  24 us (11%)
  other arithmetic  20.6 us (9%)
  between operations  14.3 us (6%)
  matrix products  13.9 us (6%)
    psum x1, waiting for transfers between devices, per_device(): extinction = lax.psum(partial, 'vox')  96.1 us
    ppermute x7, starting transfers between devices, per_device(): later.append(lax.ppermute(later[-1], 'vox', down))  18.7 us
    unnamed x63, local copies, waits for them, and re-layouts  17.5 us
    ppermute x4, starting transfers between devices, with_halo(): lax.ppermute(head, axis, [((i + 1) % count, i) for i in range(ends)])  13.4 us
    ppermute x4, waiting for transfers between devices, with_halo(): lax.ppermute(tail, axis, [(i, (i + 1) % count) for i in range(ends)])  8 us
    dot_general x1, matrix products, per_device(): jnp.einsum('sxyw,zw->sxyz', smoothed, vertical_mix, precision=HIGH)  7.82 us
    reduce_sum x1, other arithmetic, per_device(): gradient = jnp.mean(grad_latent + latent, axis=0)  6.92 us
    ppermute x4, starting transfers between devices, with_halo(): lax.ppermute(tail, axis, [(i, (i + 1) % count) for i in range(ends)])  6.91 us
  transfers between devices with their start and end apart: 24, of which 11 were waited for; matrix products, arithmetic and copies ran while one was open for 12% of the time, Pallas kernels for 0%

profile of v1, /device:TPU:10, one launch (start us, length us, event | category | flops | bytes accessed | tf_op | source)
XLA Modules:
  0.0 221.8 jit_solution(11956006830069172367)
XLA Ops:
  8.1 2.6 %collective-permute-start.12 = (f32[2,8,128]{2,1,0:T(8,128)S(1)}, f32[2,8,128]{2,1,0:T(8,128)S(1)}, u32[]{:S(2)}, u32[]{:S(2)}) collective-permute-start(f32[2,8,128]{2,1,0:T(8,128)S(1)} %pad_maximum_fusion.12), channel_id=1, source_target_pairs={{0,30},{2,0},{4,2},{6,4},{8,6},{10,8},{12,10},{14,12},{16,14},{18,... | collective-permute-start | bytes 24584 | tf_op jit(solution)/shard_map/ppermute | solution.py:77
  10.7 1.0 broadcast_add_fusion
  12.8 4.5 %collective-permute-start.1 = (f32[4,1,64,128]{3,2,1,0:T(8,128)}, f32[4,1,64,128]{3,2,1,0:T(8,128)S(1)}, u32[]{:S(2)}, u32[]{:S(2)}) collective-permute-start(f32[4,1,64,128]{3,2,1,0:T(8,128)} %get-tuple-element.19), channel_id=1, source_target_pairs={{2,0},{4,2},{6,4},{8,6},{10,8},{12,10},{14,12},{16,14},{18,16},{20... | collective-permute-start | bytes 393224 | tf_op jit(solution)/shard_map/ppermute | solution.py:19
  17.3 1.9 collective-permute-start
  19.3 1.3 compare_and_fusion.1
  20.6 2.7 %collective-permute-start.13 = (f32[2,8,128]{2,1,0:T(8,128)S(1)}, f32[2,8,128]{2,1,0:T(8,128)S(1)}, u32[]{:S(2)}, u32[]{:S(2)}) collective-permute-start(f32[2,8,128]{2,1,0:T(8,128)S(1)} %collective-permute-done.12), channel_id=1, source_target_pairs={{0,30},{2,0},{4,2},{6,4},{8,6},{10,8},{12,10},{14,12},{16,14},{18,... | collective-permute-start | bytes 24584 | tf_op jit(solution)/shard_map/ppermute | solution.py:77
  23.3 1.5 collective-permute-done.6
  25.5 2.7 %collective-permute-start.14 = (f32[2,8,128]{2,1,0:T(8,128)S(1)}, f32[2,8,128]{2,1,0:T(8,128)S(1)}, u32[]{:S(2)}, u32[]{:S(2)}) collective-permute-start(f32[2,8,128]{2,1,0:T(8,128)S(1)} %collective-permute-done.13), channel_id=1, source_target_pairs={{0,30},{2,0},{4,2},{6,4},{8,6},{10,8},{12,10},{14,12},{16,14},{18,... | collective-permute-start | bytes 24584 | tf_op jit(solution)/shard_map/ppermute | solution.py:77
  29.6 2.6 %collective-permute-start.15 = (f32[2,8,128]{2,1,0:T(8,128)S(1)}, f32[2,8,128]{2,1,0:T(8,128)S(1)}, u32[]{:S(2)}, u32[]{:S(2)}) collective-permute-start(f32[2,8,128]{2,1,0:T(8,128)S(1)} %collective-permute-done.14), channel_id=1, source_target_pairs={{0,30},{2,0},{4,2},{6,4},{8,6},{10,8},{12,10},{14,12},{16,14},{18,... | collective-permute-start | bytes 24584 | tf_op jit(solution)/shard_map/ppermute | solution.py:77
  32.8 1.7 fusion.71
  34.5 2.7 %collective-permute-start.16 = (f32[2,8,128]{2,1,0:T(8,128)S(1)}, f32[2,8,128]{2,1,0:T(8,128)}, u32[]{:S(2)}, u32[]{:S(2)}) collective-permute-start(f32[2,8,128]{2,1,0:T(8,128)S(1)} %collective-permute-done.15), channel_id=1, source_target_pairs={{0,30},{2,0},{4,2},{6,4},{8,6},{10,8},{12,10},{14,12},{16,14},{18,... | collective-permute-start | bytes 24584 | tf_op jit(solution)/shard_map/ppermute | solution.py:77
  38.6 2.7 %collective-permute-start.17 = (f32[2,8,128]{2,1,0:T(8,128)}, f32[2,8,128]{2,1,0:T(8,128)}, u32[]{:S(2)}, u32[]{:S(2)}) collective-permute-start(f32[2,8,128]{2,1,0:T(8,128)} %collective-permute-done.16), channel_id=1, source_target_pairs={{0,30},{2,0},{4,2},{6,4},{8,6},{10,8},{12,10},{14,12},{16,14},{18,... | collective-permute-start | bytes 24584 | tf_op jit(solution)/shard_map/ppermute | solution.py:77
  42.0 0.9 collective-permute-done.17
  42.9 2.7 %collective-permute-start.18 = (f32[2,8,128]{2,1,0:T(8,128)}, f32[2,8,128]{2,1,0:T(8,128)S(1)}, u32[]{:S(2)}, u32[]{:S(2)}) collective-permute-start(f32[2,8,128]{2,1,0:T(8,128)} %collective-permute-done.17), channel_id=1, source_target_pairs={{0,30},{2,0},{4,2},{6,4},{8,6},{10,8},{12,10},{14,12},{16,14},{18,... | collective-permute-start | bytes 24584 | tf_op jit(solution)/shard_map/ppermute | solution.py:77
  63.9 1.3 collective-permute-start.2
  65.2 4.5 %collective-permute-start.3 = (f32[4,4,1,128]{3,2,1,0:T(1,128)S(1)}, f32[4,4,1,128]{3,2,1,0:T(1,128)S(1)}, u32[]{:S(2)}, u32[]{:S(2)}) collective-permute-start(f32[4,4,1,128]{3,2,1,0:T(1,128)S(1)} %get-tuple-element.13), channel_id=1, source_target_pairs={{1,0},{3,2},{5,4},{7,6},{9,8},{11,10},{13,12},{15,14},{17,16},{19,... | collective-permute-start | bytes 24584 | tf_op jit(solution)/shard_map/ppermute | solution.py:19
  71.2 1.1 maximum_maximum_fusion
  72.2 7.8 %fusion.72 = (bf16[4,2,64,128]{3,2,1,0:T(8,128)(2,1)S(1)}, f32[4,2,64,128]{3,2,1,0:T(8,128)}) fusion(f32[128]{0:T(128)} %param.15, f32[128,128]{1,0:T(8,128)} %param.14, f32[4,4,65,128]{3,2,1,0:T(8,128)S(1)} %get-tuple-element.11, f32[4,1,64,128]{3,2,1,0:T(8,128)S(1)} %collective-permute-done.1, f32[4,2,64,128]{3,2,1,0:T(8,128)S(1)} %broadcast_add_fusion, ...), kind=kOutput, calls=%fused_computation.141 | convolution fusion | flops 102039552 | bytes 2556452 | tf_op jit(solution)/shard_map/sxyw,zw->sxyz/dot_general | solution.py:56
  81.0 1.8 fusion.48
  82.8 1.8 fusion.37
  86.1 96.1 %all-reduce.2.cloned.1.call-done = f32[128,4,128]{2,0,1:T(8,128)} async-done(((f32[128,4,128]{2,0,1:T(8,128)}), f32[128,4,128]{2,0,1:T(8,128)}) %all-reduce.2.cloned.1.call-update) | async-done | bytes 262160 | tf_op jit(solution)/shard_map/psum | solution.py:68
  182.1 1.7 fusion.68
  184.8 1.0 fusion.51
  186.2 1.2 fusion.32
  188.1 1.9 collective-permute-start.20
  190.0 2.4 %collective-permute-start.19 = (f32[4,1,64,128]{3,2,1,0:T(8,128)}, f32[4,1,64,128]{3,2,1,0:T(8,128)}, u32[]{:S(2)}, u32[]{:S(2)}) collective-permute-start(f32[4,1,64,128]{3,2,1,0:T(8,128)} %get-tuple-element.14), channel_id=1, source_target_pairs={{0,2},{2,4},{4,6},{6,8},{8,10},{10,12},{12,14},{14,16},{16,18},{18... | collective-permute-start | bytes 393224 | tf_op jit(solution)/shard_map/ppermute | solution.py:17
  193.2 4.4 %collective-permute-done.19 = f32[4,1,64,128]{3,2,1,0:T(8,128)} collective-permute-done((f32[4,1,64,128]{3,2,1,0:T(8,128)}, f32[4,1,64,128]{3,2,1,0:T(8,128)}, u32[]{:S(2)}, u32[]{:S(2)}) %collective-permute-start.19) | collective-permute-done | bytes 131104 | tf_op jit(solution)/shard_map/ppermute | solution.py:17
  198.3 2.5 %collective-permute-start.21 = (f32[4,4,1,128]{3,2,1,0:T(1,128)S(1)}, f32[4,4,1,128]{3,2,1,0:T(1,128)S(1)}, u32[]{:S(2)}, u32[]{:S(2)}) collective-permute-start(f32[4,4,1,128]{3,2,1,0:T(1,128)S(1)} %get-tuple-element.8), channel_id=1, source_target_pairs={{1,0},{3,2},{5,4},{7,6},{9,8},{11,10},{13,12},{15,14},{17,16},{19,... | collective-permute-start | bytes 24584 | tf_op jit(solution)/shard_map/ppermute | solution.py:19
  200.7 1.3 collective-permute-start.22
  202.6 3.6 %collective-permute-done.22 = f32[4,4,1,128]{3,2,1,0:T(1,128)S(1)} collective-permute-done((f32[4,4,1,128]{3,2,1,0:T(1,128)S(1)}, f32[4,4,1,128]{3,2,1,0:T(1,128)S(1)}, u32[]{:S(2)}, u32[]{:S(2)}) %collective-permute-start.22) | collective-permute-done | bytes 8224 | tf_op jit(solution)/shard_map/ppermute | solution.py:17
  206.3 1.1 pad_maximum_fusion.1
  207.4 6.9 %fusion.3 = f32[2,64,128]{2,1,0:T(8,128)S(1)} fusion(f32[4,4,65,128]{3,2,1,0:T(8,128)S(1)} %get-tuple-element.7, f32[4,2,64,128]{3,2,1,0:T(8,128)S(1)} %fusion.32, f32[4,1,64,128]{3,2,1,0:T(8,128)} %collective-permute-done.19, f32[4,4,65,128]{3,2,1,0:T(8,128)S(1)} %get-tuple-element.6, f32[4,1,64,128]{3,2,1,0:T(8,128)S(1)} %collective-permute-done.20, ...), kind=kLoop, calls=%fused_computation.11 | loop fusion | flops 1425408 | bytes 2490404 | tf_op jit(solution)/shard_map/reduce_sum | solution.py:110
  (113 shorter events, 33.6 us)
Async XLA Ops:
  7.2 73.8 %copy-start = (bf16[96,128,128]{2,1,0:T(8,128)(2,1)S(1)}, bf16[96,128,128]{2,1,0:T(8,128)(2,1)}, u32[]{:S(2)}) copy-start(bf16[96,128,128]{2,1,0:T(8,128)(2,1)} %param.16) | copy-start | bytes 9437188
  7.2 175.0 %all-reduce.2.cloned.1.call-start = ((), (), s32[]{:S(2)}) async-start(), calls=%async_computation | async-start | bytes 524288 | tf_op jit(solution)/shard_map/psum | solution.py:68
  8.1 4.0 %collective-permute-start.4 = (f32[2,8,128]{2,1,0:T(8,128)S(1)}, f32[2,8,128]{2,1,0:T(8,128)S(1)}, u32[]{:S(2)}, u32[]{:S(2)}) collective-permute-start(f32[2,8,128]{2,1,0:T(8,128)S(1)} %pad_maximum_fusion.12), channel_id=1, source_target_pairs={{0,2},{2,4},{4,6},{6,8},{8,10},{10,12},{12,14},{14,16},{16,18},{18... | collective-permute-start | bytes 24584 | tf_op jit(solution)/shard_map/ppermute | solution.py:75
  8.1 12.5 %collective-permute-start.12 = (f32[2,8,128]{2,1,0:T(8,128)S(1)}, f32[2,8,128]{2,1,0:T(8,128)S(1)}, u32[]{:S(2)}, u32[]{:S(2)}) collective-permute-start(f32[2,8,128]{2,1,0:T(8,128)S(1)} %pad_maximum_fusion.12), channel_id=1, source_target_pairs={{0,30},{2,0},{4,2},{6,4},{8,6},{10,8},{12,10},{14,12},{16,14},{18,... | collective-permute-start | bytes 24584 | tf_op jit(solution)/shard_map/ppermute | solution.py:77
  12.1 7.2 %collective-permute-start.5 = (f32[2,8,128]{2,1,0:T(8,128)S(1)}, f32[2,8,128]{2,1,0:T(8,128)S(1)}, u32[]{:S(2)}, u32[]{:S(2)}) collective-permute-start(f32[2,8,128]{2,1,0:T(8,128)S(1)} %collective-permute-done.4), channel_id=1, source_target_pairs={{0,2},{2,4},{4,6},{6,8},{8,10},{10,12},{12,14},{14,16},{16,18},{18... | collective-permute-start | bytes 24584 | tf_op jit(solution)/shard_map/ppermute | solution.py:75
  12.8 50.3 %collective-permute-start.1 = (f32[4,1,64,128]{3,2,1,0:T(8,128)}, f32[4,1,64,128]{3,2,1,0:T(8,128)S(1)}, u32[]{:S(2)}, u32[]{:S(2)}) collective-permute-start(f32[4,1,64,128]{3,2,1,0:T(8,128)} %get-tuple-element.19), channel_id=1, source_target_pairs={{2,0},{4,2},{6,4},{8,6},{10,8},{12,10},{14,12},{16,14},{18,16},{20... | collective-permute-start | bytes 393224 | tf_op jit(solution)/shard_map/ppermute | solution.py:19
  17.3 45.8 %collective-permute-start = (f32[4,1,64,128]{3,2,1,0:T(8,128)}, f32[4,1,64,128]{3,2,1,0:T(8,128)}, u32[]{:S(2)}, u32[]{:S(2)}) collective-permute-start(f32[4,1,64,128]{3,2,1,0:T(8,128)} %get-tuple-element.18), channel_id=1, source_target_pairs={{0,2},{2,4},{4,6},{6,8},{8,10},{10,12},{12,14},{14,16},{16,18},{18... | collective-permute-start | bytes 393224 | tf_op jit(solution)/shard_map/ppermute | solution.py:17
  19.3 6.2 %copy-start.3 = (f32[2,8,128]{2,1,0:T(8,128)}, f32[2,8,128]{2,1,0:T(8,128)S(1)}, u32[]{:S(2)}) copy-start(f32[2,8,128]{2,1,0:T(8,128)S(1)} %collective-permute-done.5) | copy-start | bytes 24580
  19.3 5.6 %collective-permute-start.6 = (f32[2,8,128]{2,1,0:T(8,128)S(1)}, f32[2,8,128]{2,1,0:T(8,128)S(1)}, u32[]{:S(2)}, u32[]{:S(2)}) collective-permute-start(f32[2,8,128]{2,1,0:T(8,128)S(1)} %collective-permute-done.5), channel_id=1, source_target_pairs={{0,2},{2,4},{4,6},{6,8},{8,10},{10,12},{12,14},{14,16},{16,18},{18... | collective-permute-start | bytes 24584 | tf_op jit(solution)/shard_map/ppermute | solution.py:75
  20.6 20.7 %copy-start.16 = (s32[96]{0:T(128)}, s32[96]{0:T(128)S(1)}, u32[]{:S(2)}) copy-start(s32[96]{0:T(128)S(1)} %get-tuple-element.3) | copy-start | bytes 1156
  20.6 4.9 %collective-permute-start.13 = (f32[2,8,128]{2,1,0:T(8,128)S(1)}, f32[2,8,128]{2,1,0:T(8,128)S(1)}, u32[]{:S(2)}, u32[]{:S(2)}) collective-permute-start(f32[2,8,128]{2,1,0:T(8,128)S(1)} %collective-permute-done.12), channel_id=1, source_target_pairs={{0,30},{2,0},{4,2},{6,4},{8,6},{10,8},{12,10},{14,12},{16,14},{18,... | collective-permute-start | bytes 24584 | tf_op jit(solution)/shard_map/ppermute | solution.py:77
  24.8 4.0 %collective-permute-start.7 = (f32[2,8,128]{2,1,0:T(8,128)S(1)}, f32[2,8,128]{2,1,0:T(8,128)S(1)}, u32[]{:S(2)}, u32[]{:S(2)}) collective-permute-start(f32[2,8,128]{2,1,0:T(8,128)S(1)} %collective-permute-done.6), channel_id=1, source_target_pairs={{0,2},{2,4},{4,6},{6,8},{8,10},{10,12},{12,14},{14,16},{16,18},{18... | collective-permute-start | bytes 24584 | tf_op jit(solution)/shard_map/ppermute | solution.py:75
  25.5 4.1 %collective-permute-start.14 = (f32[2,8,128]{2,1,0:T(8,128)S(1)}, f32[2,8,128]{2,1,0:T(8,128)S(1)}, u32[]{:S(2)}, u32[]{:S(2)}) collective-permute-start(f32[2,8,128]{2,1,0:T(8,128)S(1)} %collective-permute-done.13), channel_id=1, source_target_pairs={{0,30},{2,0},{4,2},{6,4},{8,6},{10,8},{12,10},{14,12},{16,14},{18,... | collective-permute-start | bytes 24584 | tf_op jit(solution)/shard_map/ppermute | solution.py:77
  28.8 4.0 %collective-permute-start.8 = (f32[2,8,128]{2,1,0:T(8,128)S(1)}, f32[2,8,128]{2,1,0:T(8,128)S(1)}, u32[]{:S(2)}, u32[]{:S(2)}) collective-permute-start(f32[2,8,128]{2,1,0:T(8,128)S(1)} %collective-permute-done.7), channel_id=1, source_target_pairs={{0,2},{2,4},{4,6},{6,8},{8,10},{10,12},{12,14},{14,16},{16,18},{18... | collective-permute-start | bytes 24584 | tf_op jit(solution)/shard_map/ppermute | solution.py:75
  29.6 4.9 %collective-permute-start.15 = (f32[2,8,128]{2,1,0:T(8,128)S(1)}, f32[2,8,128]{2,1,0:T(8,128)S(1)}, u32[]{:S(2)}, u32[]{:S(2)}) collective-permute-start(f32[2,8,128]{2,1,0:T(8,128)S(1)} %collective-permute-done.14), channel_id=1, source_target_pairs={{0,30},{2,0},{4,2},{6,4},{8,6},{10,8},{12,10},{14,12},{16,14},{18,... | collective-permute-start | bytes 24584 | tf_op jit(solution)/shard_map/ppermute | solution.py:77
  32.8 4.4 %collective-permute-start.9 = (f32[2,8,128]{2,1,0:T(8,128)S(1)}, f32[2,8,128]{2,1,0:T(8,128)S(1)}, u32[]{:S(2)}, u32[]{:S(2)}) collective-permute-start(f32[2,8,128]{2,1,0:T(8,128)S(1)} %collective-permute-done.8), channel_id=1, source_target_pairs={{0,2},{2,4},{4,6},{6,8},{8,10},{10,12},{12,14},{14,16},{16,18},{18... | collective-permute-start | bytes 24584 | tf_op jit(solution)/shard_map/ppermute | solution.py:75
  34.5 4.1 %collective-permute-start.16 = (f32[2,8,128]{2,1,0:T(8,128)S(1)}, f32[2,8,128]{2,1,0:T(8,128)}, u32[]{:S(2)}, u32[]{:S(2)}) collective-permute-start(f32[2,8,128]{2,1,0:T(8,128)S(1)} %collective-permute-done.15), channel_id=1, source_target_pairs={{0,30},{2,0},{4,2},{6,4},{8,6},{10,8},{12,10},{14,12},{16,14},{18,... | collective-permute-start | bytes 24584 | tf_op jit(solution)/shard_map/ppermute | solution.py:77
  37.2 4.1 %collective-permute-start.10 = (f32[2,8,128]{2,1,0:T(8,128)S(1)}, f32[2,8,128]{2,1,0:T(8,128)}, u32[]{:S(2)}, u32[]{:S(2)}) collective-permute-start(f32[2,8,128]{2,1,0:T(8,128)S(1)} %collective-permute-done.9), channel_id=1, source_target_pairs={{0,2},{2,4},{4,6},{6,8},{8,10},{10,12},{12,14},{14,16},{16,18},{18... | collective-permute-start | bytes 24584 | tf_op jit(solution)/shard_map/ppermute | solution.py:75
  38.6 4.3 %collective-permute-start.17 = (f32[2,8,128]{2,1,0:T(8,128)}, f32[2,8,128]{2,1,0:T(8,128)}, u32[]{:S(2)}, u32[]{:S(2)}) collective-permute-start(f32[2,8,128]{2,1,0:T(8,128)} %collective-permute-done.16), channel_id=1, source_target_pairs={{0,30},{2,0},{4,2},{6,4},{8,6},{10,8},{12,10},{14,12},{16,14},{18,... | collective-permute-start | bytes 24584 | tf_op jit(solution)/shard_map/ppermute | solution.py:77
  41.3 4.3 %collective-permute-start.11 = (f32[2,8,128]{2,1,0:T(8,128)}, f32[2,8,128]{2,1,0:T(8,128)}, u32[]{:S(2)}, u32[]{:S(2)}) collective-permute-start(f32[2,8,128]{2,1,0:T(8,128)} %collective-permute-done.10), channel_id=1, source_target_pairs={{0,2},{2,4},{4,6},{6,8},{8,10},{10,12},{12,14},{14,16},{16,18},{18... | collective-permute-start | bytes 24584 | tf_op jit(solution)/shard_map/ppermute | solution.py:75
  42.9 11.9 %collective-permute-start.18 = (f32[2,8,128]{2,1,0:T(8,128)}, f32[2,8,128]{2,1,0:T(8,128)S(1)}, u32[]{:S(2)}, u32[]{:S(2)}) collective-permute-start(f32[2,8,128]{2,1,0:T(8,128)} %collective-permute-done.17), channel_id=1, source_target_pairs={{0,30},{2,0},{4,2},{6,4},{8,6},{10,8},{12,10},{14,12},{16,14},{18,... | collective-permute-start | bytes 24584 | tf_op jit(solution)/shard_map/ppermute | solution.py:77
  54.7 15.7 %copy-start.10 = (f32[2,8,128]{2,1,0:T(8,128)}, f32[2,8,128]{2,1,0:T(8,128)S(1)}, u32[]{:S(2)}) copy-start(f32[2,8,128]{2,1,0:T(8,128)S(1)} %collective-permute-done.18) | copy-start | bytes 24580
  59.6 21.4 %copy-start.14 = (pred[96]{0:T(512)(128)(4,1)S(1)}, pred[96]{0:T(512)(128)(4,1)}, u32[]{:S(2)}) copy-start(pred[96]{0:T(512)(128)(4,1)} %get-tuple-element.31) | copy-start | bytes 292
  63.9 6.6 %collective-permute-start.2 = (f32[4,4,1,128]{3,2,1,0:T(1,128)S(1)}, f32[4,4,1,128]{3,2,1,0:T(1,128)S(1)}, u32[]{:S(2)}, u32[]{:S(2)}) collective-permute-start(f32[4,4,1,128]{3,2,1,0:T(1,128)S(1)} %get-tuple-element.12), channel_id=1, source_target_pairs={{0,1},{2,3},{4,5},{6,7},{8,9},{10,11},{12,13},{14,15},{16,17},{18,... | collective-permute-start | bytes 24584 | tf_op jit(solution)/shard_map/ppermute | solution.py:17
  65.2 6.0 %collective-permute-start.3 = (f32[4,4,1,128]{3,2,1,0:T(1,128)S(1)}, f32[4,4,1,128]{3,2,1,0:T(1,128)S(1)}, u32[]{:S(2)}, u32[]{:S(2)}) collective-permute-start(f32[4,4,1,128]{3,2,1,0:T(1,128)S(1)} %get-tuple-element.13), channel_id=1, source_target_pairs={{1,0},{3,2},{5,4},{7,6},{9,8},{11,10},{13,12},{15,14},{17,16},{19,... | collective-permute-start | bytes 24584 | tf_op jit(solution)/shard_map/ppermute | solution.py:19
  72.2 12.4 %copy-start.11 = (f32[2,8,128]{2,1,0:T(8,128)S(1)}, f32[2,8,128]{2,1,0:T(8,128)}, u32[]{:S(2)}) copy-start(f32[2,8,128]{2,1,0:T(8,128)} %copy-done.10) | copy-start | bytes 24580
  80.1 104.7 %copy-start.13 = (pred[96]{0:T(512)(128)(4,1)S(1)}, pred[96]{0:T(512)(128)(4,1)}, u32[]{:S(2)}) copy-start(pred[96]{0:T(512)(128)(4,1)} %get-tuple-element.2) | copy-start | bytes 292
  82.8 103.0 %copy-start.15 = (s32[96]{0:T(128)S(1)}, s32[96]{0:T(128)}, u32[]{:S(2)}) copy-start(s32[96]{0:T(128)} %param.17) | copy-start | bytes 1156
  188.1 5.1 %collective-permute-start.20 = (f32[4,1,64,128]{3,2,1,0:T(8,128)}, f32[4,1,64,128]{3,2,1,0:T(8,128)S(1)}, u32[]{:S(2)}, u32[]{:S(2)}) collective-permute-start(f32[4,1,64,128]{3,2,1,0:T(8,128)} %get-tuple-element.15), channel_id=1, source_target_pairs={{2,0},{4,2},{6,4},{8,6},{10,8},{12,10},{14,12},{16,14},{18,16},{20... | collective-permute-start | bytes 393224 | tf_op jit(solution)/shard_map/ppermute | solution.py:19
  190.0 7.5 %collective-permute-start.19 = (f32[4,1,64,128]{3,2,1,0:T(8,128)}, f32[4,1,64,128]{3,2,1,0:T(8,128)}, u32[]{:S(2)}, u32[]{:S(2)}) collective-permute-start(f32[4,1,64,128]{3,2,1,0:T(8,128)} %get-tuple-element.14), channel_id=1, source_target_pairs={{0,2},{2,4},{4,6},{6,8},{8,10},{10,12},{12,14},{14,16},{16,18},{18... | collective-permute-start | bytes 393224 | tf_op jit(solution)/shard_map/ppermute | solution.py:17
  198.3 4.4 %collective-permute-start.21 = (f32[4,4,1,128]{3,2,1,0:T(1,128)S(1)}, f32[4,4,1,128]{3,2,1,0:T(1,128)S(1)}, u32[]{:S(2)}, u32[]{:S(2)}) collective-permute-start(f32[4,4,1,128]{3,2,1,0:T(1,128)S(1)} %get-tuple-element.8), channel_id=1, source_target_pairs={{1,0},{3,2},{5,4},{7,6},{9,8},{11,10},{13,12},{15,14},{17,16},{19,... | collective-permute-start | bytes 24584 | tf_op jit(solution)/shard_map/ppermute | solution.py:19
  200.7 5.5 %collective-permute-start.22 = (f32[4,4,1,128]{3,2,1,0:T(1,128)S(1)}, f32[4,4,1,128]{3,2,1,0:T(1,128)S(1)}, u32[]{:S(2)}, u32[]{:S(2)}) collective-permute-start(f32[4,4,1,128]{3,2,1,0:T(1,128)S(1)} %get-tuple-element.9), channel_id=1, source_target_pairs={{0,1},{2,3},{4,5},{6,7},{8,9},{10,11},{12,13},{14,15},{16,17},{18,... | collective-permute-start | bytes 24584 | tf_op jit(solution)/shard_map/ppermute | solution.py:17
  (9 other events, 30.4 us)
Sparse Core Ops, SparseCore 0:
  84.7 97.3 all-reduce.1
